TPU v7x, 512 devices: a whole 4x4x16 slice. The times are simulated.
512 devices in a mesh: seq: 64 (over z, y), tensor: 8 (over x, core).
Axes of the slice: x: 4, y: 4, z: 16, core: 2. Of those that a mesh axis runs over, the one named last changes fastest.
Arguments:
- hidden: bfloat16 [8192, 4096], P('seq', 'tensor')
- norm_gain: bfloat16 [4096], replicated, may hold values from 0.5 to 1.5
- w_query: bfloat16 [4096, 4096], P('seq', 'tensor')
- key_value_weight: bfloat16 [4096, 1024], P('seq')
- w_out: bfloat16 [4096, 4096], P('tensor', 'seq'), may hold values from -0.09375 to 0.09375
- prefix_key_cache: bfloat16 [64, 1024, 1024], P('seq')
- prefix_owner: int32 [64], replicated, may hold values from 0 to 63, each once
- token_counts: int32 [64, 64], P('seq'), may hold values from 0 to 4, as said below
Outputs:
- attn_out: bfloat16 [8192, 4096], P('seq', 'tensor')
- suffix_key_cache: bfloat16 [8192, 1024], P('seq', 'tensor')
Inputs may be any that keep to these rules, and one draw needn't show every extreme that they name: `token_counts`: each row sums to 128; one prefix receives exactly 4 tokens from every sequence index.
All inputs are finite; a program needn't handle non-finite values.
Results may differ from a plain program's by a relative error of at most 0.035.
Values may be sent and summed in bfloat16 or wider, within the bound.
No kernel may reach another device: no remote copies, remote signals or barrier semaphores. Data moves between devices by JAX's collectives and lax.ppermute only.
A program may use at most 64 MiB of HBM per device.

v0:
```python
import jax
import jax.numpy as jnp
from jax import lax
from jax.sharding import PartitionSpec as P

HEAD_DIM = 128
PREFIX_LENGTH = 1024
eps = 1e-06
theta = 5000000.0


def rotate(values, positions):
    half = values.shape[-1] // 2
    frequency = theta ** (-jnp.arange(half, dtype=jnp.float32) * 2.0 / values.shape[-1])
    angle = positions.astype(jnp.float32)[:, None] * frequency[None, :]
    cosine = jnp.cos(angle)[:, None, :]
    sine = jnp.sin(angle)[:, None, :]
    first = values[..., :half]
    second = values[..., half:]
    return jnp.concatenate(
        [first * cosine - second * sine, second * cosine + first * sine], axis=-1
    )


def layout(counts_row, length):
    ends = jnp.cumsum(counts_row)
    starts = ends - counts_row
    places = jnp.arange(length, dtype=jnp.int32)
    member = (places[:, None] >= starts[None, :]) & (places[:, None] < ends[None, :])
    labels = jnp.arange(counts_row.shape[0], dtype=jnp.int32)
    prefix_group = jnp.sum(jnp.where(member, labels[None, :], 0), axis=1)
    offset = places - jnp.sum(jnp.where(member, starts[None, :], 0), axis=1)
    return (starts, prefix_group, offset)


def attend(query_vectors, keys, values, allowed):
    scores = lax.dot_general(
        query_vectors, keys, (((1,), (1,)), ((), ())), preferred_element_type=jnp.float32
    )
    scores = scores * (1.0 / query_vectors.shape[-1] ** 0.5)
    if allowed is not None:
        scores = jnp.where(allowed, scores, -1e30)
    top = jnp.max(scores, axis=1, keepdims=True)
    expo = jnp.exp(scores - top)
    total = jnp.sum(expo, axis=1, keepdims=True)
    weights = (expo / total).astype(jnp.bfloat16)
    result = jnp.dot(weights, values, preferred_element_type=jnp.float32)
    return (result, top[:, 0] + jnp.log(total[:, 0]))


def shards(
    hidden,
    norm_gain,
    w_query,
    key_value_weight,
    w_out,
    prefix_key_cache,
    prefix_owner,
    token_counts,
):
    tensor_index = lax.axis_index("tensor")
    tensor_count = lax.axis_size("tensor")
    seq_count = lax.axis_size("seq")
    length = hidden.shape[0]
    head_size = HEAD_DIM
    whole = lax.all_gather(hidden, "tensor", axis=1, tiled=True)
    wide = whole.astype(jnp.float32)
    normalized_input = (
        wide
        * lax.rsqrt(jnp.mean(wide * wide, axis=1, keepdims=True) + eps)
        * norm_gain.astype(jnp.float32)
    ).astype(jnp.bfloat16)
    width_query = w_query.shape[1]
    full_width = key_value_weight.shape[1]
    heads_dev = width_query // head_size
    kv_heads = full_width // (2 * head_size)
    group_full = heads_dev * tensor_count // kv_heads
    kv_local = max(1, heads_dev // group_full)
    kv_start = tensor_index * heads_dev // group_full
    kv_width = kv_local * 2 * head_size
    kv_piece = lax.dynamic_slice_in_dim(key_value_weight, kv_start * 2 * head_size, kv_width, 1)
    packed = jnp.concatenate([w_query, kv_piece, w_out.T], axis=1)
    gathered = lax.all_gather(packed, "seq", axis=0, tiled=True)
    wq_full = gathered[:, :width_query]
    kv_full = gathered[:, width_query : width_query + kv_width]
    wo_cols = gathered[:, width_query + kv_width :]

    def contract(piece):
        return jnp.dot(normalized_input, piece, preferred_element_type=jnp.float32)

    query_vectors = contract(wq_full)
    key_value_pair = contract(kv_full)
    counts = token_counts[0]
    num_groups = counts.shape[0]
    starts, prefix_group, offset = layout(counts, length)
    positions = PREFIX_LENGTH + offset
    query_vectors = rotate(query_vectors.reshape(length, heads_dev, head_size), positions).astype(
        jnp.bfloat16
    )
    pair_blocks = key_value_pair.reshape(length, kv_local, 2, head_size)
    rotated_keys = rotate(pair_blocks[:, :, 0], positions)
    suffix_mine = jnp.stack([rotated_keys, pair_blocks[:, :, 1]], axis=2).astype(jnp.bfloat16)
    share = full_width // tensor_count
    suffix_flat = suffix_mine.reshape(length, kv_width)
    suffix_part = lax.dynamic_slice_in_dim(
        suffix_flat, tensor_index * share - kv_start * 2 * head_size, share, 1
    )
    suffix_keys = suffix_mine[:, :, 0]
    suffix_values = suffix_mine[:, :, 1]
    cache_all = prefix_key_cache[0].reshape(-1, kv_heads, 2, head_size)
    cache_mine = lax.dynamic_slice_in_dim(cache_all, kv_start, kv_local, 1)
    cache_keys = cache_mine[:, :, 0]
    cache_values = cache_mine[:, :, 1]
    group_width = heads_dev // kv_local
    capacity = 2 * length // seq_count
    labels = jnp.arange(num_groups, dtype=jnp.int32)
    owner_match = prefix_owner[None, :] == jnp.arange(seq_count, dtype=jnp.int32)[:, None]
    owner_start = jnp.sum(jnp.where(owner_match, starts[None, :], 0), axis=1)
    owner_count = jnp.sum(jnp.where(owner_match, counts[None, :], 0), axis=1)
    slots = jnp.arange(capacity, dtype=jnp.int32)
    valid = slots[None, :] < owner_count[:, None]
    source_rows = jnp.where(valid, owner_start[:, None] + slots[None, :], 0)
    flat_query = query_vectors.reshape(length, width_query)
    outgoing = jnp.where(valid[:, :, None], flat_query[source_rows], jnp.zeros((), jnp.bfloat16))
    arrived = lax.all_to_all(outgoing, "seq", split_axis=0, concat_axis=0, tiled=True)
    items = arrived.shape[1]
    rows_in = arrived.reshape(seq_count * items, heads_dev, head_size)
    outs = []
    logs = []
    for serve_head in range(heads_dev):
        serve_result, serve_logsum = attend(
            rows_in[:, serve_head],
            cache_keys[:, serve_head // group_width],
            cache_values[:, serve_head // group_width],
            None,
        )
        outs.append(serve_result)
        logs.append(serve_logsum)
    out_block = jnp.stack(outs, axis=1).astype(jnp.bfloat16).reshape(seq_count, items, width_query)
    log_block = jnp.stack(logs, axis=1).reshape(seq_count, items, heads_dev)
    prefix_out = lax.all_to_all(out_block, "seq", split_axis=0, concat_axis=0, tiled=True)
    prefix_log = lax.all_to_all(
        log_block.astype(jnp.bfloat16), "seq", split_axis=0, concat_axis=0, tiled=True
    ).astype(log_block.dtype)
    owner_of_token = jnp.sum(
        jnp.where(prefix_group[:, None] == labels[None, :], prefix_owner[None, :], 0), axis=1
    )
    back_rows = owner_of_token * capacity + offset
    prefix_rows = prefix_out.reshape(seq_count * capacity, heads_dev, head_size)[back_rows]
    prefix_logsum = prefix_log.reshape(seq_count * capacity, heads_dev)[back_rows]
    places = jnp.arange(length, dtype=jnp.int32)
    allowed = (prefix_group[:, None] == prefix_group[None, :]) & (
        places[None, :] <= places[:, None]
    )
    outs = []
    logs = []
    for head in range(heads_dev):
        result, logsum = attend(
            query_vectors[:, head],
            suffix_keys[:, head // group_width],
            suffix_values[:, head // group_width],
            allowed,
        )
        outs.append(result)
        logs.append(logsum)
    suffix_attn = jnp.stack(outs, axis=1)
    suffix_logsum = jnp.stack(logs, axis=1)
    upper = jnp.maximum(prefix_logsum, suffix_logsum)
    left = jnp.exp(prefix_logsum - upper)[..., None]
    right = jnp.exp(suffix_logsum - upper)[..., None]
    context = (
        (left * prefix_rows.astype(jnp.float32) + right * suffix_attn) / (left + right)
    ).astype(jnp.bfloat16)
    context = context.reshape(length, width_query)
    partial_out = lax.dot_general(
        context, wo_cols, (((1,), (1,)), ((), ())), preferred_element_type=jnp.float32
    )
    attn_out = lax.psum_scatter(
        partial_out.astype(jnp.bfloat16), "tensor", scatter_dimension=1, tiled=True
    )
    return (attn_out, suffix_part)


def solution(mesh):
    in_specs = (
        P("seq", "tensor"),
        P(),
        P("seq", "tensor"),
        P("seq", None),
        P("tensor", "seq"),
        P("seq", None, None),
        P(),
        P("seq", None),
    )
    out_specs = (P("seq", "tensor"), P("seq", "tensor"))
    return jax.shard_map(shards, mesh=mesh, in_specs=in_specs, out_specs=out_specs, check_vma=False)
```

profile of v0, /device:TPU:8, one launch (start us, length us, event | category | flops | bytes accessed | tf_op | source)
XLA Modules:
  0.0 344.0 jit_solution(9256899727202618528)
XLA Ops:
  8.1 1.5 pad_maximum_fusion.1
  12.0 0.8 select_reduce_fusion.4
  13.0 2.9 copy.121
  16.6 1.0 multiply_cosine_fusion.1
  17.5 28.1 %all-gather.3.cloned.1.call-done = bf16[128,4096]{1,0:T(8,128)(2,1)} async-done(((bf16[128,512]{1,0:T(8,128)(2,1)}), bf16[128,4096]{1,0:T(8,128)(2,1)}) %all-gather.3.cloned.1.call-update) | async-done | bytes 1048592 | tf_op jit(solution)/shard_map/all_gather | solution.py:66
  45.6 1.5 fusion.3
  47.1 163.3 %all-gather.5.cloned.1.call-done = bf16[4096,1280]{1,0:T(8,128)(2,1)} async-done(((bf16[64,1280]{1,0:T(8,128)(2,1)}), bf16[4096,1280]{1,0:T(8,128)(2,1)}) %all-gather.5.cloned.1.call-update) | async-done | bytes 10485776 | tf_op jit(solution)/shard_map/all_gather | solution.py:83
  210.5 4.0 %fusion.1 = f32[128,512]{1,0:T(8,128)} fusion(bf16[4096,1280]{1,0:T(8,128)(2,1)} %all-gather.5.cloned.1.call-done, bf16[128,4096]{1,0:T(8,128)(2,1)} %all-gather.3.cloned.1.call-done, f32[4096]{0:T(1024)S(1)} %convert_element_type.81, f32[128]{0:T(128)S(1)} %add_rsqrt_fusion), kind=kOutput, calls=%fused_computation.5 | convolution fusion | flops 538968064 | bytes 5521920 | tf_op jit(solution)/shard_map/dot_general | solution.py:89
  214.5 1.0 reshape.627
  215.6 2.8 fusion.6
  218.3 1.0 reshape.633
  219.4 1.0 fusion.29
  220.6 0.9 multiply_subtract_fusion
  222.0 1.2 gather_fusion
  223.2 0.9 broadcast_select_fusion
  224.1 10.2 %all-to-all-start = ((bf16[64,4,512]{2,1,0:T(4,128)(2,1)}), bf16[64,4,512]{2,1,0:T(4,128)(2,1)S(1)}, u32[]{:S(2)}, u32[]{:S(2)}) async-start(bf16[64,4,512]{2,1,0:T(4,128)(2,1)} %broadcast_select_fusion), calls=%async_computation | async-start | bytes 524288 | tf_op jit(solution)/shard_map/all_to_all | solution.py:125
  235.3 16.7 %all-to-all-done = bf16[64,4,512]{2,1,0:T(4,128)(2,1)S(1)} async-done(((bf16[64,4,512]{2,1,0:T(4,128)(2,1)}), bf16[64,4,512]{2,1,0:T(4,128)(2,1)S(1)}, u32[]{:S(2)}, u32[]{:S(2)}) %all-to-all-start) | async-done | bytes 262176 | tf_op jit(solution)/shard_map/all_to_all | solution.py:125
  258.0 5.4 %all-to-all-start.1 = ((bf16[64,4,4]{1,2,0:T(4,128)(2,1)}), bf16[64,4,4]{1,2,0:T(4,128)(2,1)S(1)}, u32[]{:S(2)}, u32[]{:S(2)}) async-start(bf16[64,4,4]{1,2,0:T(4,128)(2,1)} %copy.123), calls=%async_computation.1 | async-start | bytes 131072 | tf_op jit(solution)/shard_map/all_to_all | solution.py:142
  263.7 0.8 convert_element_type.91
  264.6 13.0 %all-to-all-done.1 = bf16[64,4,4]{1,2,0:T(4,128)(2,1)S(1)} async-done(((bf16[64,4,4]{1,2,0:T(4,128)(2,1)}), bf16[64,4,4]{1,2,0:T(4,128)(2,1)S(1)}, u32[]{:S(2)}, u32[]{:S(2)}) %all-to-all-start.1) | async-done | bytes 2080 | tf_op jit(solution)/shard_map/all_to_all | solution.py:142
  277.6 5.5 %all-to-all-start.2 = ((bf16[64,4,512]{2,1,0:T(4,128)(2,1)}), bf16[64,4,512]{2,1,0:T(4,128)(2,1)S(1)}, u32[]{:S(2)}, u32[]{:S(2)}) async-start(bf16[64,4,512]{2,1,0:T(4,128)(2,1)} %convert_element_type.91), calls=%async_computation.2 | async-start | bytes 524288 | tf_op jit(solution)/shard_map/all_to_all | solution.py:141
  284.7 16.4 %all-to-all-done.2 = bf16[64,4,512]{2,1,0:T(4,128)(2,1)S(1)} async-done(((bf16[64,4,512]{2,1,0:T(4,128)(2,1)}), bf16[64,4,512]{2,1,0:T(4,128)(2,1)S(1)}, u32[]{:S(2)}, u32[]{:S(2)}) %all-to-all-start.2) | async-done | bytes 262176 | tf_op jit(solution)/shard_map/all_to_all | solution.py:141
  302.2 4.7 %convolution_convert_fusion = bf16[128,4096]{1,0:T(8,128)(2,1)} fusion(bf16[128,512]{0,1:T(8,128)(2,1)S(1)} %bitcast.161, bf16[4096,1280]{1,0:T(8,128)(2,1)} %all-gather.5.cloned.1.call-done), kind=kOutput, calls=%fused_computation.3 | convolution fusion | flops 537395200 | bytes 5373952 | tf_op jit(solution)/shard_map/dot_general | solution.py:175
  307.7 29.7 %reduce-scatter.2.cloned.1.call-done = bf16[128,512]{1,0:T(8,128)(2,1)} async-done(((bf16[128,4096]{1,0:T(8,128)(2,1)}), bf16[128,512]{1,0:T(8,128)(2,1)}) %reduce-scatter.2.cloned.1.call-update) | async-done | bytes 131088 | tf_op jit(solution)/shard_map/reduce_scatter | solution.py:178
  (100 shorter events, 15.5 us)
Async XLA Ops:
  7.2 0.9 copy-start
  7.2 38.4 %all-gather.3.cloned.1.call-start = ((), (), s32[]{:S(2)}) async-start(), calls=%async_computation.4 | async-start | bytes 1179648 | tf_op jit(solution)/shard_map/all_gather | solution.py:66
  7.9 202.5 %all-gather.5.cloned.1.call-start = ((), (), s32[]{:S(2)}) async-start(), calls=%async_computation.5 | async-start | bytes 10649600 | tf_op jit(solution)/shard_map/all_gather | solution.py:83
  10.3 200.1 %copy-start.2 = (f32[4096]{0:T(1024)}, f32[4096]{0:T(1024)S(1)}, u32[]{:S(2)}) copy-start(f32[4096]{0:T(1024)S(1)} %convert_element_type.81) | copy-start | bytes 49156
  13.0 3.0 copy-start.5
  15.9 194.6 %copy-start.3 = (f32[64]{0:T(128)}, f32[64]{0:T(128)S(1)}, u32[]{:S(2)}) copy-start(f32[64]{0:T(128)S(1)} %multiply_power_fusion) | copy-start | bytes 772
  16.0 0.6 copy-start.6
  16.1 194.3 %copy-start.4 = (f32[128]{0:T(128)}, f32[128]{0:T(128)S(1)}, u32[]{:S(2)}) copy-start(f32[128]{0:T(128)S(1)} %add_convert_fusion.4) | copy-start | bytes 1540
  47.1 163.4 %copy-start.8 = (f32[128]{0:T(128)}, f32[128]{0:T(128)S(1)}, u32[]{:S(2)}) copy-start(f32[128]{0:T(128)S(1)} %add_rsqrt_fusion) | copy-start | bytes 1540
  47.1 168.4 %copy-start.1 = (bf16[128,4096]{1,0:T(8,128)(2,1)S(1)}, bf16[128,4096]{1,0:T(8,128)(2,1)}, u32[]{:S(2)}) copy-start(bf16[128,4096]{1,0:T(8,128)(2,1)} %all-gather.3.cloned.1.call-done) | copy-start | bytes 3145732
  218.3 3.5 %copy-start.7 = (s32[128]{0:T(128)S(1)}, s32[128]{0:T(128)}, u32[]{:S(2)}) copy-start(s32[128]{0:T(128)} %copy-done.6) | copy-start | bytes 1540
  224.1 27.9 %all-to-all-start = ((bf16[64,4,512]{2,1,0:T(4,128)(2,1)}), bf16[64,4,512]{2,1,0:T(4,128)(2,1)S(1)}, u32[]{:S(2)}, u32[]{:S(2)}) async-start(bf16[64,4,512]{2,1,0:T(4,128)(2,1)} %broadcast_select_fusion), calls=%async_computation | async-start | bytes 524288 | tf_op jit(solution)/shard_map/all_to_all | solution.py:125
  258.0 19.6 %all-to-all-start.1 = ((bf16[64,4,4]{1,2,0:T(4,128)(2,1)}), bf16[64,4,4]{1,2,0:T(4,128)(2,1)S(1)}, u32[]{:S(2)}, u32[]{:S(2)}) async-start(bf16[64,4,4]{1,2,0:T(4,128)(2,1)} %copy.123), calls=%async_computation.1 | async-start | bytes 131072 | tf_op jit(solution)/shard_map/all_to_all | solution.py:142
  277.6 23.5 %all-to-all-start.2 = ((bf16[64,4,512]{2,1,0:T(4,128)(2,1)}), bf16[64,4,512]{2,1,0:T(4,128)(2,1)S(1)}, u32[]{:S(2)}, u32[]{:S(2)}) async-start(bf16[64,4,512]{2,1,0:T(4,128)(2,1)} %convert_element_type.91), calls=%async_computation.2 | async-start | bytes 524288 | tf_op jit(solution)/shard_map/all_to_all | solution.py:141
  283.1 54.3 %reduce-scatter.2.cloned.1.call-start = ((), (), s32[]{:S(2)}) async-start(), calls=%async_computation.6 | async-start | bytes 1179648 | tf_op jit(solution)/shard_map/reduce_scatter | solution.py:178
Sparse Core Ops, SparseCore 0:
  10.1 35.3 all-gather.2
  48.5 161.8 all-gather.4
  307.0 30.4 reduce-scatter.1
where the time goes:
time: 345 us; the launch traced here: 344 us
  waiting for transfers between devices  268 us (78%)
  starting transfers between devices  21.3 us (6%)
  matrix products  16 us (5%)
  between operations  14.2 us (4%)
  local copies, waits for them, and re-layouts  13.2 us (4%)
  other arithmetic  11.4 us (3%)
    all_gather x1, waiting for transfers between devices, shards(): gathered = lax.all_gather(packed, 'seq', axis=0, tiled=True)  163 us
    reduce_scatter x1, waiting for transfers between devices, shards(): lax.psum_scatter(partial_out.astype(jnp.bfloat16), 'tensor', scatter_dime...  29.7 us
    all_gather x1, waiting for transfers between devices, shards(): whole = lax.all_gather(hidden, 'tensor', axis=1, tiled=True)  28.1 us
    all_to_all x1, waiting for transfers between devices, shards(): lax.all_to_all(outgoing, 'seq', split_axis=0, concat_axis=0, tiled=True)  16.7 us
    all_to_all x1, waiting for transfers between devices, shards(): lax.all_to_all(out_block, 'seq', split_axis=0, concat_axis=0, tiled=True)  16.4 us
    all_to_all x1, waiting for transfers between devices, shards(): lax.all_to_all(log_block.astype(jnp.bfloat16), 'seq', split_axis=0, conca...  13 us
    all_to_all x1, starting transfers between devices, shards(): lax.all_to_all(outgoing, 'seq', split_axis=0, concat_axis=0, tiled=True)  10.2 us
  transfers between devices with their start and end apart: 6, of which 6 were waited for; matrix products, arithmetic and copies ran while one was open for 4% of the time, Pallas kernels for 0%

commit v1 on v0

--- a/solution.py
+++ b/solution.py
@@ -7,6 +7,24 @@
 PREFIX_LENGTH = 1024
 eps = 1e-06
 theta = 5000000.0
+
+
+def collect(shard, axis, dim):
+    ways, here, step = (lax.axis_size(axis), lax.axis_index(axis), shard.shape[dim])
+    lengths = [n * ways if d == dim else n for d, n in enumerate(shard.shape)]
+    full = lax.dynamic_update_slice_in_dim(
+        jnp.zeros(lengths, shard.dtype), shard, here * step, axis=dim
+    )
+    going_up = going_down = shard
+    for far in range(1, ways // 2 + 1):
+        going_up = lax.ppermute(going_up, axis, [(d, (d + 1) % ways) for d in range(ways)])
+        full = lax.dynamic_update_slice_in_dim(full, going_up, (here - far) % ways * step, axis=dim)
+        if 2 * far < ways:
+            going_down = lax.ppermute(going_down, axis, [(d, (d - 1) % ways) for d in range(ways)])
+            full = lax.dynamic_update_slice_in_dim(
+                full, going_down, (here + far) % ways * step, axis=dim
+            )
+    return full
 
 
 def rotate(values, positions):
@@ -63,7 +81,7 @@
     seq_count = lax.axis_size("seq")
     length = hidden.shape[0]
     head_size = HEAD_DIM
-    whole = lax.all_gather(hidden, "tensor", axis=1, tiled=True)
+    whole = collect(hidden, "tensor", 1)
     wide = whole.astype(jnp.float32)
     normalized_input = (
         wide

time: 345 us -> 312 us (0.904)
  waiting for transfers between devices: 268 us -> 225 us
  starting transfers between devices: 21.3 us -> 29.6 us
    all_gather x1 -> x0, waiting for transfers between devices: 28.1 us -> none  [shards(): whole = lax.all_gather(hidden, 'tensor', axis=1, tiled=True)]
    all_gather x1, waiting for transfers between devices: 163 us -> 136 us  [shards(): gathered = lax.all_gather(packed, 'seq', axis=0, tiled=True)]
    ppermute x0 -> x7, waiting for transfers between devices: none -> 13 us  [the longest x4 11.1 us: collect(): lax.ppermute(going_up, axis, [(d, (d + 1) % ways) for d in range(ways)])]
    ppermute x0 -> x7, starting transfers between devices: none -> 8.16 us  [the longest x3 8.15 us: collect(): lax.ppermute(going_down, axis, [(d, (d - 1) % ways) for d in range(ways)])]
  transfers between devices with their start and end apart: 6 -> 12, of which waited for: 6 -> 8; matrix products, arithmetic and copies ran while one was open for 4% -> 5% of each run, Pallas kernels for 0% -> 0%
where the time goes in v1:
time: 312 us; the launch traced here: 311 us
  waiting for transfers between devices  225 us (72%)
  starting transfers between devices  29.6 us (9%)
  matrix products  15.7 us (5%)
  local copies, waits for them, and re-layouts  14.7 us (5%)
  between operations  14.6 us (5%)
  other arithmetic  11.5 us (4%)
    all_gather x1, waiting for transfers between devices, shards(): gathered = lax.all_gather(packed, 'seq', axis=0, tiled=True)  136 us
    reduce_scatter x1, waiting for transfers between devices, shards(): lax.psum_scatter(partial_out.astype(jnp.bfloat16), 'tensor', scatter_dime...  29.7 us
    all_to_all x1, waiting for transfers between devices, shards(): lax.all_to_all(outgoing, 'seq', split_axis=0, concat_axis=0, tiled=True)  16.7 us
    all_to_all x1, waiting for transfers between devices, shards(): lax.all_to_all(out_block, 'seq', split_axis=0, concat_axis=0, tiled=True)  16.4 us
    all_to_all x1, waiting for transfers between devices, shards(): lax.all_to_all(log_block.astype(jnp.bfloat16), 'seq', split_axis=0, conca...  13 us
    ppermute x4, waiting for transfers between devices, collect(): lax.ppermute(going_up, axis, [(d, (d + 1) % ways) for d in range(ways)])  11.1 us
    all_to_all x1, starting transfers between devices, shards(): lax.all_to_all(outgoing, 'seq', split_axis=0, concat_axis=0, tiled=True)  10.2 us
    ppermute x3, starting transfers between devices, collect(): lax.ppermute(going_down, axis, [(d, (d - 1) % ways) for d in range(ways)])  8.15 us
  transfers between devices with their start and end apart: 12, of which 8 were waited for; matrix products, arithmetic and copies ran while one was open for 5% of the time, Pallas kernels for 0%

profile of v1, /device:TPU:8, one launch (start us, length us, event | category | flops | bytes accessed | tf_op | source)
XLA Modules:
  0.0 311.1 jit_solution(1847677353461532612)
XLA Ops:
  8.1 1.5 pad_maximum_fusion.1
  9.7 2.2 collective-permute-start.1
  15.5 1.0 multiply_cosine_fusion.1
  16.5 1.3 convert_element_type.81
  17.8 2.9 copy.121
  20.9 3.0 collective-permute-start.3
  24.8 1.9 collective-permute-done.3
  26.7 3.0 collective-permute-start.5
  29.7 5.6 %collective-permute-done.4 = bf16[128,512]{1,0:T(8,128)(2,1)S(1)} collective-permute-done((bf16[128,512]{1,0:T(8,128)(2,1)S(1)}, bf16[128,512]{1,0:T(8,128)(2,1)S(1)}, u32[]{:S(2)}, u32[]{:S(2)}) %collective-permute-start.4) | collective-permute-done | bytes 131104 | tf_op jit(solution)/shard_map/ppermute | solution.py:20
  35.3 5.5 %collective-permute-done.6 = bf16[128,512]{1,0:T(8,128)(2,1)S(1)} collective-permute-done((bf16[128,512]{1,0:T(8,128)(2,1)S(1)}, bf16[128,512]{1,0:T(8,128)(2,1)S(1)}, u32[]{:S(2)}, u32[]{:S(2)}) %collective-permute-start.6) | collective-permute-done | bytes 131104 | tf_op jit(solution)/shard_map/ppermute | solution.py:20
  41.2 136.2 %all-gather.2.cloned.1.call-done = bf16[4096,1280]{1,0:T(8,128)(2,1)} async-done(((bf16[64,1280]{1,0:T(8,128)(2,1)}), bf16[4096,1280]{1,0:T(8,128)(2,1)}) %all-gather.2.cloned.1.call-update) | async-done | bytes 10485776 | tf_op jit(solution)/shard_map/all_gather | solution.py:101
  177.4 3.7 %fusion.1 = f32[128,512]{1,0:T(8,128)} fusion(bf16[4096,1280]{1,0:T(8,128)(2,1)} %all-gather.2.cloned.1.call-done, bf16[128,4096]{1,0:T(8,128)(2,1)S(1)} %constant_dynamic-update-slice_fusion, f32[4096]{0:T(1024)} %convert_element_type.81, f32[128]{0:T(128)S(1)} %add_rsqrt_fusion), kind=kOutput, calls=%fused_computation.5 | convolution fusion | flops 538968064 | bytes 5521920 | tf_op jit(solution)/shard_map/dot_general | solution.py:107
  181.1 1.0 reshape.627
  182.1 2.8 fusion.6
  186.0 1.0 fusion.29
  188.6 1.2 gather_fusion
  190.7 10.2 %all-to-all-start = ((bf16[64,4,512]{2,1,0:T(4,128)(2,1)}), bf16[64,4,512]{2,1,0:T(4,128)(2,1)S(1)}, u32[]{:S(2)}, u32[]{:S(2)}) async-start(bf16[64,4,512]{2,1,0:T(4,128)(2,1)} %broadcast_select_fusion), calls=%async_computation | async-start | bytes 524288 | tf_op jit(solution)/shard_map/all_to_all | solution.py:143
  202.0 16.7 %all-to-all-done = bf16[64,4,512]{2,1,0:T(4,128)(2,1)S(1)} async-done(((bf16[64,4,512]{2,1,0:T(4,128)(2,1)}), bf16[64,4,512]{2,1,0:T(4,128)(2,1)S(1)}, u32[]{:S(2)}, u32[]{:S(2)}) %all-to-all-start) | async-done | bytes 262176 | tf_op jit(solution)/shard_map/all_to_all | solution.py:143
  224.7 5.5 %all-to-all-start.1 = ((bf16[64,4,4]{1,2,0:T(4,128)(2,1)}), bf16[64,4,4]{1,2,0:T(4,128)(2,1)S(1)}, u32[]{:S(2)}, u32[]{:S(2)}) async-start(bf16[64,4,4]{1,2,0:T(4,128)(2,1)} %copy.123), calls=%async_computation.1 | async-start | bytes 131072 | tf_op jit(solution)/shard_map/all_to_all | solution.py:160
  231.2 13.0 %all-to-all-done.1 = bf16[64,4,4]{1,2,0:T(4,128)(2,1)S(1)} async-done(((bf16[64,4,4]{1,2,0:T(4,128)(2,1)}), bf16[64,4,4]{1,2,0:T(4,128)(2,1)S(1)}, u32[]{:S(2)}, u32[]{:S(2)}) %all-to-all-start.1) | async-done | bytes 2080 | tf_op jit(solution)/shard_map/all_to_all | solution.py:160
  244.2 5.7 %all-to-all-start.2 = ((bf16[64,4,512]{2,1,0:T(4,128)(2,1)}), bf16[64,4,512]{2,1,0:T(4,128)(2,1)S(1)}, u32[]{:S(2)}, u32[]{:S(2)}) async-start(bf16[64,4,512]{2,1,0:T(4,128)(2,1)} %convert_element_type.91), calls=%async_computation.2 | async-start | bytes 524288 | tf_op jit(solution)/shard_map/all_to_all | solution.py:159
  251.6 16.4 %all-to-all-done.2 = bf16[64,4,512]{2,1,0:T(4,128)(2,1)S(1)} async-done(((bf16[64,4,512]{2,1,0:T(4,128)(2,1)}), bf16[64,4,512]{2,1,0:T(4,128)(2,1)S(1)}, u32[]{:S(2)}, u32[]{:S(2)}) %all-to-all-start.2) | async-done | bytes 262176 | tf_op jit(solution)/shard_map/all_to_all | solution.py:159
  269.0 4.7 %convolution_convert_fusion = bf16[128,4096]{1,0:T(8,128)(2,1)} fusion(bf16[128,512]{0,1:T(8,128)(2,1)S(1)} %bitcast.161, bf16[4096,1280]{1,0:T(8,128)(2,1)} %all-gather.2.cloned.1.call-done), kind=kOutput, calls=%fused_computation.3 | convolution fusion | flops 537395200 | bytes 5373952 | tf_op jit(solution)/shard_map/dot_general | solution.py:193
  274.6 29.7 %reduce-scatter.2.cloned.1.call-done = bf16[128,512]{1,0:T(8,128)(2,1)} async-done(((bf16[128,4096]{1,0:T(8,128)(2,1)}), bf16[128,512]{1,0:T(8,128)(2,1)}) %reduce-scatter.2.cloned.1.call-update) | async-done | bytes 131088 | tf_op jit(solution)/shard_map/reduce_scatter | solution.py:196
  (116 shorter events, 21.0 us)
Async XLA Ops:
  7.2 0.9 copy-start
  7.2 170.2 %all-gather.2.cloned.1.call-start = ((), (), s32[]{:S(2)}) async-start(), calls=%async_computation.4 | async-start | bytes 10649600 | tf_op jit(solution)/shard_map/all_gather | solution.py:101
  9.7 11.2 %collective-permute-start.1 = (bf16[128,512]{1,0:T(8,128)(2,1)}, bf16[128,512]{1,0:T(8,128)(2,1)}, u32[]{:S(2)}, u32[]{:S(2)}) collective-permute-start(bf16[128,512]{1,0:T(8,128)(2,1)} %param.8), channel_id=1, source_target_pairs={{0,7},{1,0},{2,1},{3,2},{4,3},{5,4},{6,5},{7,6},{8,15},{9,8},{10,9... | collective-permute-start | bytes 393224 | tf_op jit(solution)/shard_map/ppermute | solution.py:23
  11.9 12.0 %collective-permute-start = (bf16[128,512]{1,0:T(8,128)(2,1)}, bf16[128,512]{1,0:T(8,128)(2,1)S(1)}, u32[]{:S(2)}, u32[]{:S(2)}) collective-permute-start(bf16[128,512]{1,0:T(8,128)(2,1)} %param.8), channel_id=1, source_target_pairs={{0,1},{1,2},{2,3},{3,4},{4,5},{5,6},{6,7},{7,0},{8,9},{9,10},{10,1... | collective-permute-start | bytes 393224 | tf_op jit(solution)/shard_map/ppermute | solution.py:20
  14.5 2.0 copy-start.2
  14.6 1.9 copy-start.4
  15.4 1.1 copy-start.3
  17.8 3.1 copy-start.1
  20.9 5.8 %collective-permute-start.3 = (bf16[128,512]{1,0:T(8,128)(2,1)}, bf16[128,512]{1,0:T(8,128)(2,1)S(1)}, u32[]{:S(2)}, u32[]{:S(2)}) collective-permute-start(bf16[128,512]{1,0:T(8,128)(2,1)} %collective-permute-done.1), channel_id=1, source_target_pairs={{0,7},{1,0},{2,1},{3,2},{4,3},{5,4},{6,5},{7,6},{8,15},{9,8},{10,9... | collective-permute-start | bytes 393224 | tf_op jit(solution)/shard_map/ppermute | solution.py:23
  23.8 5.8 %collective-permute-start.2 = (bf16[128,512]{1,0:T(8,128)(2,1)S(1)}, bf16[128,512]{1,0:T(8,128)(2,1)S(1)}, u32[]{:S(2)}, u32[]{:S(2)}) collective-permute-start(bf16[128,512]{1,0:T(8,128)(2,1)S(1)} %collective-permute-done), channel_id=1, source_target_pairs={{0,1},{1,2},{2,3},{3,4},{4,5},{5,6},{6,7},{7,0},{8,9},{9,10},{10,1... | collective-permute-start | bytes 393224 | tf_op jit(solution)/shard_map/ppermute | solution.py:20
  26.7 8.6 %collective-permute-start.5 = (bf16[128,512]{1,0:T(8,128)(2,1)S(1)}, bf16[128,512]{1,0:T(8,128)(2,1)S(1)}, u32[]{:S(2)}, u32[]{:S(2)}) collective-permute-start(bf16[128,512]{1,0:T(8,128)(2,1)S(1)} %collective-permute-done.3), channel_id=1, source_target_pairs={{0,7},{1,0},{2,1},{3,2},{4,3},{5,4},{6,5},{7,6},{8,15},{9,8},{10,9... | collective-permute-start | bytes 393224 | tf_op jit(solution)/shard_map/ppermute | solution.py:23
  29.7 5.6 %collective-permute-start.4 = (bf16[128,512]{1,0:T(8,128)(2,1)S(1)}, bf16[128,512]{1,0:T(8,128)(2,1)S(1)}, u32[]{:S(2)}, u32[]{:S(2)}) collective-permute-start(bf16[128,512]{1,0:T(8,128)(2,1)S(1)} %collective-permute-done.2), channel_id=1, source_target_pairs={{0,1},{1,2},{2,3},{3,4},{4,5},{5,6},{6,7},{7,0},{8,9},{9,10},{10,1... | collective-permute-start | bytes 393224 | tf_op jit(solution)/shard_map/ppermute | solution.py:20
  35.3 5.6 %collective-permute-start.6 = (bf16[128,512]{1,0:T(8,128)(2,1)S(1)}, bf16[128,512]{1,0:T(8,128)(2,1)S(1)}, u32[]{:S(2)}, u32[]{:S(2)}) collective-permute-start(bf16[128,512]{1,0:T(8,128)(2,1)S(1)} %collective-permute-done.4), channel_id=1, source_target_pairs={{0,1},{1,2},{2,3},{3,4},{4,5},{5,6},{6,7},{7,0},{8,9},{9,10},{10,1... | collective-permute-start | bytes 393224 | tf_op jit(solution)/shard_map/ppermute | solution.py:20
  41.2 136.2 %copy-start.6 = (f32[128]{0:T(128)}, f32[128]{0:T(128)S(1)}, u32[]{:S(2)}) copy-start(f32[128]{0:T(128)S(1)} %add_rsqrt_fusion) | copy-start | bytes 1540
  184.9 3.5 %copy-start.5 = (s32[128]{0:T(128)S(1)}, s32[128]{0:T(128)}, u32[]{:S(2)}) copy-start(s32[128]{0:T(128)} %copy-done.4) | copy-start | bytes 1540
  190.7 27.9 %all-to-all-start = ((bf16[64,4,512]{2,1,0:T(4,128)(2,1)}), bf16[64,4,512]{2,1,0:T(4,128)(2,1)S(1)}, u32[]{:S(2)}, u32[]{:S(2)}) async-start(bf16[64,4,512]{2,1,0:T(4,128)(2,1)} %broadcast_select_fusion), calls=%async_computation | async-start | bytes 524288 | tf_op jit(solution)/shard_map/all_to_all | solution.py:143
  224.7 19.6 %all-to-all-start.1 = ((bf16[64,4,4]{1,2,0:T(4,128)(2,1)}), bf16[64,4,4]{1,2,0:T(4,128)(2,1)S(1)}, u32[]{:S(2)}, u32[]{:S(2)}) async-start(bf16[64,4,4]{1,2,0:T(4,128)(2,1)} %copy.123), calls=%async_computation.1 | async-start | bytes 131072 | tf_op jit(solution)/shard_map/all_to_all | solution.py:160
  244.2 23.7 %all-to-all-start.2 = ((bf16[64,4,512]{2,1,0:T(4,128)(2,1)}), bf16[64,4,512]{2,1,0:T(4,128)(2,1)S(1)}, u32[]{:S(2)}, u32[]{:S(2)}) async-start(bf16[64,4,512]{2,1,0:T(4,128)(2,1)} %convert_element_type.91), calls=%async_computation.2 | async-start | bytes 524288 | tf_op jit(solution)/shard_map/all_to_all | solution.py:159
  250.0 54.3 %reduce-scatter.2.cloned.1.call-start = ((), (), s32[]{:S(2)}) async-start(), calls=%async_computation.5 | async-start | bytes 1179648 | tf_op jit(solution)/shard_map/reduce_scatter | solution.py:196
Sparse Core Ops, SparseCore 0:
  11.0 166.3 all-gather.1
  273.8 30.4 reduce-scatter.1
